TPU v7x, 512 devices: a whole 4x4x16 slice. The times are simulated.
512 devices in a mesh: dp: 8 (over x, y_hi), expert: 64 (over y_lo, z, core).
Axes of the slice: x: 4, y: 4 (y_hi: 2, y_lo: 2; y = y_hi * 2 + y_lo), z: 16, core: 2. Of those that a mesh axis runs over, the one named last changes fastest.
Arguments:
- tokens: bfloat16 [65536, 2048], P(('dp', 'expert')), may hold values from -6 to 6
- out_grad: bfloat16 [65536, 2048], P(('dp', 'expert')), may hold values from -6 to 6
- combine: float32 [65536, 2], P(('dp', 'expert')), may hold values from 0.1 to 1
- expert_ids: int32 [65536, 2], P(('dp', 'expert')), may hold values from 0 to 63, all different within a row; in each aligned block of 128 rows (0 to 127, 128 to 255, ...) at most 5 rows name the same one
- gate_weight: bfloat16 [64, 2048, 768], P('expert', 'dp'), may hold values from -0.125 to 0.125
- up_weight: bfloat16 [64, 2048, 768], P('expert', 'dp'), may hold values from -0.125 to 0.125
- down_weight: bfloat16 [64, 2048, 768], P('expert', 'dp'), may hold values from -0.21875 to 0.21875
Outputs:
- token_grad: bfloat16 [65536, 2048], P(('dp', 'expert'))
- down_grad: bfloat16 [64, 2048, 768], P('expert', 'dp')
Inputs may be any that keep to these rules, and one draw needn't show every extreme that they name: `expert_ids`: each row names 2 different experts. Among the 128 rows of one device no expert is named more than 5 times, a bound that some block reaches.
All inputs are finite; a program needn't handle non-finite values.
Results may differ from a plain program's by a relative error of at most 0.012.
Values may be sent and summed in bfloat16 or wider, within the bound.
No kernel may reach another device: no remote copies, remote signals or barrier semaphores. Data moves between devices by JAX's collectives and lax.ppermute only.
A program may use at most 64 MiB of HBM per device.

v0:
```python
import jax
import jax.numpy as jnp
from jax import lax
from jax.sharding import Mesh
from jax.sharding import PartitionSpec as P

TOP = 2
CAP = 5
SUB = ("ylo", "z", "core")
ROWS = ("dp",) + SUB


def local_then_z(x, kinds):
    x = lax.all_to_all(x, "core", 3, 3, tiled=True)
    x = lax.all_to_all(x, "ylo", 1, 1, tiled=True)
    return [lax.all_to_all(x[k], "z", 1, 1, tiled=True) for k in range(kinds)]


def z_then_local(x):
    x = lax.all_to_all(x, "z", 1, 1, tiled=True)
    x = lax.all_to_all(x, "ylo", 0, 0, tiled=True)
    return lax.all_to_all(x, "core", 2, 2, tiled=True)


def body(tokens, out_grad, combine, expert_ids, gate_weight, up_weight, down_weight):
    token_rows = tokens.shape[0]
    width = tokens.shape[1]
    n_ylo, n_z, n_core = (lax.axis_size(a) for a in SUB)
    expert_count = n_ylo * n_z * n_core
    capacity = CAP
    positions = expert_count * capacity
    w_gate = lax.all_gather(gate_weight, "dp", axis=1, tiled=True)[0]
    w_up = lax.all_gather(up_weight, "dp", axis=1, tiled=True)[0]
    w_down = lax.all_gather(down_weight, "dp", axis=1, tiled=True)[0]
    flat_ids = expert_ids.reshape(-1)
    onehot = (flat_ids[:, None] == jnp.arange(expert_count, dtype=jnp.int32)[None, :]).astype(
        jnp.int32
    )
    earlier = jnp.cumsum(onehot, axis=0) - onehot
    slot_index = jnp.sum(earlier * onehot, axis=1)
    target = flat_ids * capacity + slot_index
    matches = target[None, :] == jnp.arange(positions, dtype=jnp.int32)[:, None]
    picker = jnp.sum(
        matches.reshape(positions, token_rows, TOP).astype(jnp.float32), axis=2
    ).astype(jnp.bfloat16)
    slot_weight = jnp.sum(
        jnp.where(matches, combine.reshape(-1)[None, :], jnp.float32(0.0)), axis=1
    )
    row_send = jnp.dot(picker, tokens, preferred_element_type=jnp.float32).astype(jnp.bfloat16)
    picked_grad = jnp.dot(picker, out_grad, preferred_element_type=jnp.float32)
    grad_send = (slot_weight[:, None] * picked_grad).astype(jnp.bfloat16)
    send = jnp.stack([row_send, grad_send]).reshape(2, n_ylo, n_z, n_core, capacity, width)
    rows_in, grads_in = local_then_z(send, 2)
    rows_in = rows_in.reshape(positions, width)
    grads_in = grads_in.reshape(positions, width)
    gate_pre = jnp.dot(rows_in, w_gate, preferred_element_type=jnp.float32)
    up_pre = jnp.dot(rows_in, w_up, preferred_element_type=jnp.float32)
    sigmoid_gate = jax.nn.sigmoid(gate_pre)
    silu_gate = gate_pre * sigmoid_gate
    hidden = (silu_gate * up_pre).astype(jnp.bfloat16)
    hidden_grad = jnp.dot(grads_in, w_down, preferred_element_type=jnp.float32)
    gate_grad = (
        hidden_grad * up_pre * sigmoid_gate * (1.0 + gate_pre * (1.0 - sigmoid_gate))
    ).astype(jnp.bfloat16)
    up_grad = (hidden_grad * silu_gate).astype(jnp.bfloat16)
    contract_hidden = (((1,), (1,)), ((), ()))
    row_grad = (
        lax.dot_general(gate_grad, w_gate, contract_hidden, preferred_element_type=jnp.float32)
        + lax.dot_general(up_grad, w_up, contract_hidden, preferred_element_type=jnp.float32)
    ).astype(jnp.bfloat16)
    back_rows = z_then_local(row_grad.reshape(n_ylo, n_z, n_core, capacity, width))
    token_grad = lax.dot_general(
        picker,
        back_rows.reshape(positions, width),
        (((0,), (0,)), ((), ())),
        preferred_element_type=jnp.float32,
    ).astype(jnp.bfloat16)
    down_grad = lax.psum_scatter(
        lax.dot_general(
            grads_in, hidden, (((0,), (0,)), ((), ())), preferred_element_type=jnp.float32
        ).astype(jnp.bfloat16),
        "dp",
        scatter_dimension=0,
        tiled=True,
    )
    return (token_grad, down_grad[None])


def solution(mesh):
    n_dp, n_expert = mesh.devices.shape
    fine = Mesh(mesh.devices.reshape(n_dp, 2, n_expert // 4, 2), ("dp",) + SUB)
    rows = P(ROWS, None)
    weights = P(SUB, "dp", None)
    return jax.shard_map(
        body,
        mesh=fine,
        in_specs=(rows, rows, rows, rows, weights, weights, weights),
        out_specs=(rows, weights),
        check_vma=False,
    )
```

profile of v0, /device:TPU:33, one launch (start us, length us, event | category | flops | bytes accessed | tf_op | source)
XLA Modules:
  0.0 378.4 jit_solution(1346013559021178343)
XLA Ops:
  12.0 1.6 fusion.16
  13.6 2.4 stack.10
  16.0 1.6 convolution_convert_fusion.1
  17.6 3.4 stack.9
  21.0 2.5 pad_maximum_fusion
  23.5 1.7 copy.54
  25.3 6.1 %all_to_all.35 = bf16[2,2,16,2,5,2048]{5,2,4,1,0,3:T(8,128)(2,1)S(1)} all-to-all(bf16[2,2,16,2,5,2048]{5,2,4,1,0,3:T(8,128)(2,1)S(1)} %copy.54), channel_id=1, replica_groups=mesh['dp'=8,'ylo'=2,'z'=16,'core'=2] {'core'}, dimensions={3} | all-to-all | bytes 5242880 | tf_op jit(solution)/shard_map/all_to_all | solution.py:14
  31.8 38.4 %all_to_all.36 = bf16[2,2,16,2,5,2048]{5,2,4,3,0,1:T(8,128)(2,1)S(1)} all-to-all(bf16[2,2,16,2,5,2048]{5,2,4,3,0,1:T(8,128)(2,1)S(1)} %copy.55), channel_id=1, replica_groups=mesh['dp'=8,'ylo'=2,'z'=16,'core'=2] {'ylo'}, dimensions={1} | all-to-all | bytes 5242880 | tf_op jit(solution)/shard_map/all_to_all | solution.py:15
  70.4 2.4 copy.58
  72.8 12.2 %all-to-all-start.3 = ((bf16[2,16,2,5,2048]{4,2,3,0,1:T(2,128)(2,1)}), bf16[2,16,2,5,2048]{4,2,3,0,1:T(2,128)(2,1)S(1)}, u32[]{:S(2)}, u32[]{:S(2)}) async-start(bf16[2,16,2,5,2048]{4,2,3,0,1:T(2,128)(2,1)} %copy.58), calls=%async_computation.3 | async-start | bytes 2621440 | tf_op jit(solution)/shard_map/all_to_all | solution.py:16
  85.7 2.4 copy.56
  88.1 53.9 %all-to-all-done.3 = bf16[2,16,2,5,2048]{4,2,3,0,1:T(2,128)(2,1)S(1)} async-done(((bf16[2,16,2,5,2048]{4,2,3,0,1:T(2,128)(2,1)}), bf16[2,16,2,5,2048]{4,2,3,0,1:T(2,128)(2,1)S(1)}, u32[]{:S(2)}, u32[]{:S(2)}) %all-to-all-start.3) | async-done | bytes 1310752 | tf_op jit(solution)/shard_map/all_to_all | solution.py:16
  142.0 12.2 %all-to-all-start.2 = ((bf16[2,16,2,5,2048]{4,2,3,0,1:T(2,128)(2,1)}), bf16[2,16,2,5,2048]{4,2,3,0,1:T(2,128)(2,1)}, u32[]{:S(2)}, u32[]{:S(2)}) async-start(bf16[2,16,2,5,2048]{4,2,3,0,1:T(2,128)(2,1)} %copy.56), calls=%async_computation.2 | async-start | bytes 2621440 | tf_op jit(solution)/shard_map/all_to_all | solution.py:16
  155.2 2.0 copy.59
  157.2 1.4 reshape.61
  158.7 52.2 %all-to-all-done.2 = bf16[2,16,2,5,2048]{4,2,3,0,1:T(2,128)(2,1)} async-done(((bf16[2,16,2,5,2048]{4,2,3,0,1:T(2,128)(2,1)}), bf16[2,16,2,5,2048]{4,2,3,0,1:T(2,128)(2,1)}, u32[]{:S(2)}, u32[]{:S(2)}) %all-to-all-start.2) | async-done | bytes 1310752 | tf_op jit(solution)/shard_map/all_to_all | solution.py:16
  210.8 2.0 copy.57
  212.9 1.4 reshape.60
  214.3 4.6 %fusion.2 = f32[320,768]{1,0:T(8,128)} fusion(bf16[320,2048]{1,0:T(8,128)(2,1)} %reshape.61, bf16[1,2048,768]{2,1,0:T(8,128)(2,1)} %all-gather.8.cloned.1.call-done), kind=kOutput, calls=%fused_computation.4 | convolution fusion | flops 1006632960 | bytes 5439488 | tf_op jit(solution)/shard_map/dot_general | solution.py:56
  218.9 3.2 fusion.6
  223.1 3.6 convolution_convert_fusion
  226.7 29.6 %all-gather.4.cloned.1.call-done = bf16[1,2048,768]{2,1,0:T(8,128)(2,1)} async-done(((bf16[1,256,768]{2,1,0:T(8,128)(2,1)}), bf16[1,2048,768]{2,1,0:T(8,128)(2,1)}) %all-gather.4.cloned.1.call-update) | async-done | bytes 3145744 | tf_op jit(solution)/shard_map/all_gather | solution.py:34
  256.3 3.2 fusion.8
  259.5 1.3 fusion
  261.4 2.3 fusion.13
  263.7 2.4 reshape.62
  266.1 1.5 copy.60
  267.6 74.4 %all_to_all.37 = bf16[2,16,2,5,2048]{4,2,3,0,1:T(2,128)(2,1)S(1)} all-to-all(bf16[2,16,2,5,2048]{4,2,3,0,1:T(2,128)(2,1)S(1)} %copy.60), channel_id=1, replica_groups=mesh['dp'=8,'ylo'=2,'z'=16,'core'=2] {'z'}, dimensions={1} | all-to-all | bytes 2621440 | tf_op jit(solution)/shard_map/all_to_all | solution.py:20
  342.7 17.1 %all_to_all.38 = bf16[2,16,2,5,2048]{4,1,3,2,0:T(8,128)(2,1)S(1)} all-to-all(bf16[2,16,2,5,2048]{4,1,3,2,0:T(8,128)(2,1)S(1)} %copy.61), channel_id=1, replica_groups=mesh['dp'=8,'ylo'=2,'z'=16,'core'=2] {'ylo'}, dimensions={0} | all-to-all | bytes 2621440 | tf_op jit(solution)/shard_map/all_to_all | solution.py:21
  360.0 7.2 %all_to_all.39 = bf16[2,16,2,5,2048]{4,1,3,0,2:T(8,128)(2,1)S(1)} all-to-all(bf16[2,16,2,5,2048]{4,1,3,0,2:T(8,128)(2,1)S(1)} %copy.62), channel_id=1, replica_groups=mesh['dp'=8,'ylo'=2,'z'=16,'core'=2] {'core'}, dimensions={2} | all-to-all | bytes 2621440 | tf_op jit(solution)/shard_map/all_to_all | solution.py:22
  367.9 1.4 reshape.63
  369.3 2.6 convolution_convert_fusion.2
  (57 shorter events, 10.1 us)
Async XLA Ops:
  7.2 4.8 %copy-start = (bf16[128,2048]{1,0:T(8,128)(2,1)S(1)}, bf16[128,2048]{1,0:T(8,128)(2,1)}, u32[]{:S(2)}) copy-start(bf16[128,2048]{1,0:T(8,128)(2,1)} %param.8) | copy-start | bytes 1572868
  7.2 207.1 %all-gather.8.cloned.1.call-start = ((), (), s32[]{:S(2)}) async-start(), calls=%async_computation.10 | async-start | bytes 3538944 | tf_op jit(solution)/shard_map/all_gather | solution.py:32
  13.6 2.4 copy-start.5
  72.8 69.2 %all-to-all-start.3 = ((bf16[2,16,2,5,2048]{4,2,3,0,1:T(2,128)(2,1)}), bf16[2,16,2,5,2048]{4,2,3,0,1:T(2,128)(2,1)S(1)}, u32[]{:S(2)}, u32[]{:S(2)}) async-start(bf16[2,16,2,5,2048]{4,2,3,0,1:T(2,128)(2,1)} %copy.58), calls=%async_computation.3 | async-start | bytes 2621440 | tf_op jit(solution)/shard_map/all_to_all | solution.py:16
  85.0 133.9 %all-gather.6.cloned.1.call-start = ((), (), s32[]{:S(2)}) async-start(), calls=%async_computation.9 | async-start | bytes 3538944 | tf_op jit(solution)/shard_map/all_gather | solution.py:33
  142.0 12.9 %copy-start.2 = (bf16[2,16,2,5,2048]{4,2,3,0,1:T(2,128)(2,1)}, bf16[2,16,2,5,2048]{4,2,3,0,1:T(2,128)(2,1)S(1)}, u32[]{:S(2)}) copy-start(bf16[2,16,2,5,2048]{4,2,3,0,1:T(2,128)(2,1)S(1)} %all-to-all-done.3) | copy-start | bytes 3932164
  142.0 68.8 %all-to-all-start.2 = ((bf16[2,16,2,5,2048]{4,2,3,0,1:T(2,128)(2,1)}), bf16[2,16,2,5,2048]{4,2,3,0,1:T(2,128)(2,1)}, u32[]{:S(2)}, u32[]{:S(2)}) async-start(bf16[2,16,2,5,2048]{4,2,3,0,1:T(2,128)(2,1)} %copy.56), calls=%async_computation.2 | async-start | bytes 2621440 | tf_op jit(solution)/shard_map/all_to_all | solution.py:16
  154.3 102.0 %all-gather.4.cloned.1.call-start = ((), (), s32[]{:S(2)}) async-start(), calls=%async_computation.8 | async-start | bytes 3538944 | tf_op jit(solution)/shard_map/all_gather | solution.py:34
  155.0 216.9 %reduce-scatter.2.cloned.1.call-start = ((), (), s32[]{:S(2)}) async-start(), calls=%async_computation.11 | async-start | bytes 3538944 | tf_op jit(solution)/shard_map/reduce_scatter | solution.py:78
  214.3 4.6 %copy-start.4 = (bf16[320,2048]{1,0:T(8,128)(2,1)S(1)}, bf16[320,2048]{1,0:T(8,128)(2,1)}, u32[]{:S(2)}) copy-start(bf16[320,2048]{1,0:T(8,128)(2,1)} %reshape.61) | copy-start | bytes 3932164
  218.9 4.2 %copy-start.3 = (bf16[320,2048]{1,0:T(8,128)(2,1)S(1)}, bf16[320,2048]{1,0:T(8,128)(2,1)}, u32[]{:S(2)}) copy-start(bf16[320,2048]{1,0:T(8,128)(2,1)} %reshape.60) | copy-start | bytes 3932164
  218.9 4.2 %copy-start.8 = (f32[320,768]{1,0:T(8,128)S(1)}, f32[320,768]{1,0:T(8,128)}, u32[]{:S(2)}) copy-start(f32[320,768]{1,0:T(8,128)} %fusion.2) | copy-start | bytes 2949124
  222.1 0.9 copy-start.10
  226.7 32.8 %copy-start.9 = (f32[320,768]{1,0:T(8,128)S(1)}, f32[320,768]{1,0:T(8,128)}, u32[]{:S(2)}) copy-start(f32[320,768]{1,0:T(8,128)} %fusion.2) | copy-start | bytes 2949124
  256.3 3.2 copy-start.6
  256.3 3.2 copy-start.11
  259.5 1.9 copy-start.7
  367.1 4.8 %copy-start.1 = (bf16[128,2048]{1,0:T(8,128)(2,1)S(1)}, bf16[128,2048]{1,0:T(8,128)(2,1)}, u32[]{:S(2)}) copy-start(bf16[128,2048]{1,0:T(8,128)(2,1)} %param.8) | copy-start | bytes 1572868
Sparse Core Ops, SparseCore 0:
  11.2 85.0 all-gather.7
  99.4 76.5 all-gather.5
  179.2 77.0 all-gather.3
  261.5 94.4 reduce-scatter.1
where the time goes:
time: 379 us; the launch traced here: 378 us
  blocking collectives  143 us (38%)
  waiting for transfers between devices  138 us (36%)
  local copies, waits for them, and re-layouts  30.6 us (8%)
  starting transfers between devices  24.7 us (7%)
  matrix products  24 us (6%)
  between operations  14 us (4%)
  other arithmetic  4.2 us (1%)
    all_to_all x2, waiting for transfers between devices, local_then_z(): return [lax.all_to_all(x[k], 'z', 1, 1, tiled=True) for k in range(kinds)]  106 us
    all_to_all x1, blocking collectives, z_then_local(): x = lax.all_to_all(x, 'z', 1, 1, tiled=True)  74.4 us
    all_to_all x1, blocking collectives, local_then_z(): x = lax.all_to_all(x, 'ylo', 1, 1, tiled=True)  38.4 us
    all_gather x1, waiting for transfers between devices, body(): w_down = lax.all_gather(down_weight, 'dp', axis=1, tiled=True)[0]  29.6 us
    all_to_all x2, starting transfers between devices, local_then_z(): return [lax.all_to_all(x[k], 'z', 1, 1, tiled=True) for k in range(kinds)]  24.4 us
    all_to_all x1, blocking collectives, z_then_local(): x = lax.all_to_all(x, 'ylo', 0, 0, tiled=True)  17.1 us
  transfers between devices with their start and end apart: 6, of which 3 were waited for; matrix products, arithmetic and copies ran while one was open for 15% of the time, Pallas kernels for 0%

commit v1 on v0

--- a/solution.py
+++ b/solution.py
@@ -31,7 +31,9 @@
     positions = expert_count * capacity
     w_gate = lax.all_gather(gate_weight, "dp", axis=1, tiled=True)[0]
     w_up = lax.all_gather(up_weight, "dp", axis=1, tiled=True)[0]
-    w_down = lax.all_gather(down_weight, "dp", axis=1, tiled=True)[0]
+    w_down = jnp.concatenate(
+        lax.all_to_all(jnp.stack([down_weight] * lax.axis_size("dp")), "dp", 0, 0), axis=1
+    )[0]
     flat_ids = expert_ids.reshape(-1)
     onehot = (flat_ids[:, None] == jnp.arange(expert_count, dtype=jnp.int32)[None, :]).astype(
         jnp.int32

time: 379 us -> 410 us (1.082)
  waiting for transfers between devices: 138 us -> 159 us
  starting transfers between devices: 24.7 us -> 33.9 us
  blocking collectives: 143 us -> 137 us
    all_to_all x0 -> x1, waiting for transfers between devices: none -> 38.5 us  [body(): lax.all_to_all(jnp.stack([down_weight] * lax.axis_size('dp')), 'dp', 0, 0)]
    all_gather x1 -> x0, waiting for transfers between devices: 29.6 us -> none  [body(): w_down = lax.all_gather(down_weight, 'dp', axis=1, tiled=True)[0]]
    all_gather x1, waiting for transfers between devices: 0.01 us -> 9.5 us  [body(): w_up = lax.all_gather(up_weight, 'dp', axis=1, tiled=True)[0]]
    all_to_all x0 -> x1, starting transfers between devices: none -> 6.63 us  [body(): lax.all_to_all(jnp.stack([down_weight] * lax.axis_size('dp')), 'dp', 0, 0)]
    all_to_all x1, blocking collectives: 38.4 us -> 32.7 us  [local_then_z(): x = lax.all_to_all(x, 'ylo', 1, 1, tiled=True)]
  transfers between devices with their start and end apart: 6 -> 6, of which waited for: 3 -> 4; matrix products, arithmetic and copies ran while one was open for 15% -> 9% of each run, Pallas kernels for 0% -> 0%
where the time goes in v1:
time: 410 us; the launch traced here: 409 us
  waiting for transfers between devices  159 us (39%)
  blocking collectives  137 us (33%)
  local copies, waits for them, and re-layouts  34 us (8%)
  starting transfers between devices  33.9 us (8%)
  matrix products  27 us (7%)
  between operations  13.9 us (3%)
  other arithmetic  4.2 us (1%)
    all_to_all x2, waiting for transfers between devices, local_then_z(): return [lax.all_to_all(x[k], 'z', 1, 1, tiled=True) for k in range(kinds)]  110 us
    all_to_all x1, blocking collectives, z_then_local(): x = lax.all_to_all(x, 'z', 1, 1, tiled=True)  74.1 us
    all_to_all x1, waiting for transfers between devices, body(): lax.all_to_all(jnp.stack([down_weight] * lax.axis_size('dp')), 'dp', 0, 0)  38.5 us
    all_to_all x1, blocking collectives, local_then_z(): x = lax.all_to_all(x, 'ylo', 1, 1, tiled=True)  32.7 us
    all_to_all x2, starting transfers between devices, local_then_z(): return [lax.all_to_all(x[k], 'z', 1, 1, tiled=True) for k in range(kinds)]  27 us
    all_to_all x1, blocking collectives, z_then_local(): x = lax.all_to_all(x, 'ylo', 0, 0, tiled=True)  17.1 us
    all_gather x1, waiting for transfers between devices, body(): w_up = lax.all_gather(up_weight, 'dp', axis=1, tiled=True)[0]  9.5 us
  transfers between devices with their start and end apart: 6, of which 4 were waited for; matrix products, arithmetic and copies ran while one was open for 9% of the time, Pallas kernels for 0%

profile of v1, /device:TPU:33, one launch (start us, length us, event | category | flops | bytes accessed | tf_op | source)
XLA Modules:
  0.0 409.2 jit_solution(7696508327362618709)
XLA Ops:
  11.3 1.6 fusion.14
  12.9 2.4 stack.9
  15.3 1.6 convolution_convert_fusion.1
  16.9 3.4 stack.8
  20.3 2.5 pad_maximum_fusion
  22.8 1.7 copy.54
  24.6 6.1 %all_to_all.40 = bf16[2,2,16,2,5,2048]{5,2,4,1,0,3:T(8,128)(2,1)S(1)} all-to-all(bf16[2,2,16,2,5,2048]{5,2,4,1,0,3:T(8,128)(2,1)S(1)} %copy.54), channel_id=1, replica_groups=mesh['dp'=8,'ylo'=2,'z'=16,'core'=2] {'core'}, dimensions={3} | all-to-all | bytes 5242880 | tf_op jit(solution)/shard_map/all_to_all | solution.py:14
  31.0 32.7 %all_to_all.41 = bf16[2,2,16,2,5,2048]{5,2,4,3,0,1:T(8,128)(2,1)S(1)} all-to-all(bf16[2,2,16,2,5,2048]{5,2,4,3,0,1:T(8,128)(2,1)S(1)} %copy.55), channel_id=1, replica_groups=mesh['dp'=8,'ylo'=2,'z'=16,'core'=2] {'ylo'}, dimensions={1} | all-to-all | bytes 5242880 | tf_op jit(solution)/shard_map/all_to_all | solution.py:15
  64.0 2.4 copy.58
  66.5 14.6 %all-to-all-start.4 = ((bf16[2,16,2,5,2048]{4,2,3,0,1:T(2,128)(2,1)}), bf16[2,16,2,5,2048]{4,2,3,0,1:T(2,128)(2,1)S(1)}, u32[]{:S(2)}, u32[]{:S(2)}) async-start(bf16[2,16,2,5,2048]{4,2,3,0,1:T(2,128)(2,1)} %copy.58), calls=%async_computation.4 | async-start | bytes 2621440 | tf_op jit(solution)/shard_map/all_to_all | solution.py:16
  81.8 2.4 copy.56
  84.3 53.9 %all-to-all-done.4 = bf16[2,16,2,5,2048]{4,2,3,0,1:T(2,128)(2,1)S(1)} async-done(((bf16[2,16,2,5,2048]{4,2,3,0,1:T(2,128)(2,1)}), bf16[2,16,2,5,2048]{4,2,3,0,1:T(2,128)(2,1)S(1)}, u32[]{:S(2)}, u32[]{:S(2)}) %all-to-all-start.4) | async-done | bytes 1310752 | tf_op jit(solution)/shard_map/all_to_all | solution.py:16
  138.2 12.3 %all-to-all-start.2 = ((bf16[2,16,2,5,2048]{4,2,3,0,1:T(2,128)(2,1)}), bf16[2,16,2,5,2048]{4,2,3,0,1:T(2,128)(2,1)S(1)}, u32[]{:S(2)}, u32[]{:S(2)}) async-start(bf16[2,16,2,5,2048]{4,2,3,0,1:T(2,128)(2,1)} %copy.56), calls=%async_computation.2 | async-start | bytes 2621440 | tf_op jit(solution)/shard_map/all_to_all | solution.py:16
  151.2 55.7 %all-to-all-done.2 = bf16[2,16,2,5,2048]{4,2,3,0,1:T(2,128)(2,1)S(1)} async-done(((bf16[2,16,2,5,2048]{4,2,3,0,1:T(2,128)(2,1)}), bf16[2,16,2,5,2048]{4,2,3,0,1:T(2,128)(2,1)S(1)}, u32[]{:S(2)}, u32[]{:S(2)}) %all-to-all-start.2) | async-done | bytes 1310752 | tf_op jit(solution)/shard_map/all_to_all | solution.py:16
  207.0 2.0 stack.11
  209.0 6.6 %all-to-all-start.3 = ((bf16[8,1,256,768]{3,2,1,0:T(8,128)(2,1)}), bf16[8,1,256,768]{3,2,1,0:T(8,128)(2,1)}, u32[]{:S(2)}, u32[]{:S(2)}) async-start(bf16[8,1,256,768]{3,2,1,0:T(8,128)(2,1)} %stack.11), calls=%async_computation.3 | async-start | bytes 6291456 | tf_op jit(solution)/shard_map/all_to_all | solution.py:35
  215.9 2.3 copy.59
  219.6 2.0 copy.57
  223.0 38.5 %all-to-all-done.3 = bf16[8,1,256,768]{3,2,1,0:T(8,128)(2,1)} async-done(((bf16[8,1,256,768]{3,2,1,0:T(8,128)(2,1)}), bf16[8,1,256,768]{3,2,1,0:T(8,128)(2,1)}, u32[]{:S(2)}, u32[]{:S(2)}) %all-to-all-start.3) | async-done | bytes 3145760 | tf_op jit(solution)/shard_map/all_to_all | solution.py:35
  261.6 4.5 %fusion.29 = f32[320,768]{1,0:T(8,128)} fusion(bf16[320,2048]{1,0:T(8,128)(2,1)} %reshape.63, bf16[2048,768]{1,0:T(8,128)(2,1)} %bitcast.3), kind=kOutput, calls=%fused_computation.45 | convolution fusion | flops 1006632960 | bytes 5439488 | tf_op jit(solution)/shard_map/dot_general | solution.py:63
  266.1 4.0 fusion.2
  270.1 9.5 %all-gather.3.cloned.1.call-done = bf16[1,2048,768]{2,1,0:T(8,128)(2,1)} async-done(((bf16[1,256,768]{2,1,0:T(8,128)(2,1)}), bf16[1,2048,768]{2,1,0:T(8,128)(2,1)}) %all-gather.3.cloned.1.call-update) | async-done | bytes 3145744 | tf_op jit(solution)/shard_map/all_gather | solution.py:33
  279.6 3.1 fusion.6
  283.7 3.7 convolution_convert_fusion
  288.9 3.6 fusion
  292.6 2.3 fusion.11
  294.9 2.4 reshape.65
  297.2 1.5 copy.60
  298.8 74.1 %all_to_all.42 = bf16[2,16,2,5,2048]{4,2,3,0,1:T(2,128)(2,1)S(1)} all-to-all(bf16[2,16,2,5,2048]{4,2,3,0,1:T(2,128)(2,1)S(1)} %copy.60), channel_id=1, replica_groups=mesh['dp'=8,'ylo'=2,'z'=16,'core'=2] {'z'}, dimensions={1} | all-to-all | bytes 2621440 | tf_op jit(solution)/shard_map/all_to_all | solution.py:20
  373.6 17.1 %all_to_all.43 = bf16[2,16,2,5,2048]{4,1,3,2,0:T(8,128)(2,1)S(1)} all-to-all(bf16[2,16,2,5,2048]{4,1,3,2,0:T(8,128)(2,1)S(1)} %copy.61), channel_id=1, replica_groups=mesh['dp'=8,'ylo'=2,'z'=16,'core'=2] {'ylo'}, dimensions={0} | all-to-all | bytes 2621440 | tf_op jit(solution)/shard_map/all_to_all | solution.py:21
  390.8 7.2 %all_to_all.44 = bf16[2,16,2,5,2048]{4,1,3,0,2:T(8,128)(2,1)S(1)} all-to-all(bf16[2,16,2,5,2048]{4,1,3,0,2:T(8,128)(2,1)S(1)} %copy.62), channel_id=1, replica_groups=mesh['dp'=8,'ylo'=2,'z'=16,'core'=2] {'core'}, dimensions={2} | all-to-all | bytes 2621440 | tf_op jit(solution)/shard_map/all_to_all | solution.py:22
  400.1 2.6 convolution_convert_fusion.2
  (59 shorter events, 14.7 us)
Async XLA Ops:
  7.2 4.2 %copy-start = (bf16[128,2048]{1,0:T(8,128)(2,1)S(1)}, bf16[128,2048]{1,0:T(8,128)(2,1)}, u32[]{:S(2)}) copy-start(bf16[128,2048]{1,0:T(8,128)(2,1)} %param.8) | copy-start | bytes 1572868
  12.9 2.4 copy-start.6
  66.5 71.7 %all-to-all-start.4 = ((bf16[2,16,2,5,2048]{4,2,3,0,1:T(2,128)(2,1)}), bf16[2,16,2,5,2048]{4,2,3,0,1:T(2,128)(2,1)S(1)}, u32[]{:S(2)}, u32[]{:S(2)}) async-start(bf16[2,16,2,5,2048]{4,2,3,0,1:T(2,128)(2,1)} %copy.58), calls=%async_computation.4 | async-start | bytes 2621440 | tf_op jit(solution)/shard_map/all_to_all | solution.py:16
  81.1 184.9 %all-gather.5.cloned.1.call-start = ((), (), s32[]{:S(2)}) async-start(), calls=%async_computation.10 | async-start | bytes 3538944 | tf_op jit(solution)/shard_map/all_gather | solution.py:32
  84.3 122.7 %copy-start.7 = (bf16[1,256,768]{2,1,0:T(8,128)(2,1)S(1)}, bf16[1,256,768]{2,1,0:T(8,128)(2,1)}, u32[]{:S(2)}) copy-start(bf16[1,256,768]{2,1,0:T(8,128)(2,1)} %param.13) | copy-start | bytes 1179652
  138.2 70.8 %copy-start.2 = (bf16[2,16,2,5,2048]{4,2,3,0,1:T(2,128)(2,1)}, bf16[2,16,2,5,2048]{4,2,3,0,1:T(2,128)(2,1)S(1)}, u32[]{:S(2)}) copy-start(bf16[2,16,2,5,2048]{4,2,3,0,1:T(2,128)(2,1)S(1)} %all-to-all-done.4) | copy-start | bytes 3932164
  138.2 68.8 %all-to-all-start.2 = ((bf16[2,16,2,5,2048]{4,2,3,0,1:T(2,128)(2,1)}), bf16[2,16,2,5,2048]{4,2,3,0,1:T(2,128)(2,1)S(1)}, u32[]{:S(2)}, u32[]{:S(2)}) async-start(bf16[2,16,2,5,2048]{4,2,3,0,1:T(2,128)(2,1)} %copy.56), calls=%async_computation.2 | async-start | bytes 2621440 | tf_op jit(solution)/shard_map/all_to_all | solution.py:16
  150.5 129.1 %all-gather.3.cloned.1.call-start = ((), (), s32[]{:S(2)}) async-start(), calls=%async_computation.9 | async-start | bytes 3538944 | tf_op jit(solution)/shard_map/all_gather | solution.py:33
  207.0 2.0 copy-start.3
  209.0 52.5 %all-to-all-start.3 = ((bf16[8,1,256,768]{3,2,1,0:T(8,128)(2,1)}), bf16[8,1,256,768]{3,2,1,0:T(8,128)(2,1)}, u32[]{:S(2)}, u32[]{:S(2)}) async-start(bf16[8,1,256,768]{3,2,1,0:T(8,128)(2,1)} %stack.11), calls=%async_computation.3 | async-start | bytes 6291456 | tf_op jit(solution)/shard_map/all_to_all | solution.py:35
  215.7 187.1 %reduce-scatter.2.cloned.1.call-start = ((), (), s32[]{:S(2)}) async-start(), calls=%async_computation.11 | async-start | bytes 3538944 | tf_op jit(solution)/shard_map/reduce_scatter | solution.py:80
  261.5 4.5 %copy-start.4 = (bf16[320,2048]{1,0:T(8,128)(2,1)S(1)}, bf16[320,2048]{1,0:T(8,128)(2,1)}, u32[]{:S(2)}) copy-start(bf16[320,2048]{1,0:T(8,128)(2,1)} %reshape.64) | copy-start | bytes 3932164
  270.1 13.6 %copy-start.5 = (bf16[320,2048]{1,0:T(8,128)(2,1)S(1)}, bf16[320,2048]{1,0:T(8,128)(2,1)}, u32[]{:S(2)}) copy-start(bf16[320,2048]{1,0:T(8,128)(2,1)} %reshape.63) | copy-start | bytes 3932164
  279.6 4.1 %copy-start.10 = (f32[320,768]{1,0:T(8,128)S(1)}, f32[320,768]{1,0:T(8,128)}, u32[]{:S(2)}) copy-start(f32[320,768]{1,0:T(8,128)} %fusion.2) | copy-start | bytes 2949124
  282.8 1.0 copy-start.12
  287.4 1.2 copy-start.9
  287.4 1.5 copy-start.11
  288.9 3.7 copy-start.8
  398.0 4.8 %copy-start.1 = (bf16[128,2048]{1,0:T(8,128)(2,1)S(1)}, bf16[128,2048]{1,0:T(8,128)(2,1)}, u32[]{:S(2)}) copy-start(bf16[128,2048]{1,0:T(8,128)(2,1)} %param.8) | copy-start | bytes 1572868
Sparse Core Ops, SparseCore 0:
  85.1 80.1 all-gather.4
  168.5 111.0 all-gather.2
  287.5 91.9 reduce-scatter.1
